TPU v7x, 32 devices: a whole 2x2x4 slice. The times are simulated.
32 devices in a mesh: nets: 8 (over z, x), region: 4 (over y, core).
Axes of the slice: x: 2, y: 2, z: 4, core: 2. Of those that a mesh axis runs over, the one named last changes fastest.
Arguments:
- logits: float32 [8192, 256], P('nets'), may hold values from -24 to 465
- tile_values: bfloat16 [8, 4, 384, 128, 128], P('nets', 'region'), may hold values from 0 to 1
- tile_pattern: int32 [8, 4, 384], P('nets', 'region'), may hold values from 0 to 2047
- tile_edge: int32 [8, 4, 384], P('nets', 'region'), may hold values from 0 to 63
- tile_counts: int32 [8, 4, 8], P('nets', 'region'), may hold values from 12 to 48, as said below
- capacity: int32 [4, 65536], P('region', 'nets'), may hold values from 0 to 2
Outputs:
- logit_grad: float32 [8192, 256], P('nets')
- usage: float32 [4, 65536], P('region', 'nets')
Inputs may be any that keep to these rules, and one draw needn't show every extreme that they name: `tile_counts`: each entry is at most 48; in every draw some owner receives 48 live slots from every group of a region, and every group has a full owner in every region.
All inputs are finite; a program needn't handle non-finite values.
Results may differ from a plain program's by a relative error of at most 0.0011.
Values may be sent and summed in bfloat16 or wider, within the bound.
No kernel may reach another device: no remote copies, remote signals or barrier semaphores. Data moves between devices by JAX's collectives and lax.ppermute only.
A program may use at most 64 MiB of HBM per device.

v0:
```python
import jax
import jax.numpy as jnp
from jax import lax
from jax.sharding import PartitionSpec as P


def shards(logits, tile_values, tile_pattern, tile_edge, tile_counts, capacity):
    groups = lax.axis_size("nets")
    tile_block = tile_values[0, 0]
    tile_count = tile_block.shape[0]
    block_size = tile_block.shape[1]
    slot_count = tile_count // groups
    pattern_idx = tile_pattern[0, 0]
    edge_idx = tile_edge[0, 0]
    counts = tile_counts[0, 0]
    live_slot = (jnp.arange(slot_count, dtype=jnp.int32)[None, :] < counts[:, None]).reshape(
        tile_count
    )
    weight_live = live_slot.astype(jnp.float32)
    probs = jax.nn.softmax(logits, axis=-1)
    probs_half = probs.astype(jnp.bfloat16).reshape(-1, block_size)
    picked = probs_half[pattern_idx]
    contrib = (
        jnp.einsum("tq,tqe->te", picked, tile_block, preferred_element_type=jnp.float32)
        * weight_live[:, None]
    )
    capacity_f = capacity.reshape(-1, block_size).astype(jnp.float32)
    owned_blocks = capacity_f.shape[0]
    owner_idx = jnp.arange(tile_count, dtype=jnp.int32) // slot_count
    target = owner_idx * owned_blocks + edge_idx
    partial_value = (
        jnp.zeros((groups * owned_blocks, block_size), jnp.float32).at[target].add(contrib)
    )
    usage_edges = lax.psum_scatter(partial_value, "nets", scatter_dimension=0, tiled=True)
    edge_grad = jax.nn.sigmoid(usage_edges - capacity_f).astype(jnp.bfloat16)
    all_grads = lax.all_gather(edge_grad, "nets", axis=0, tiled=True)
    slot_grads = all_grads[target]
    dp_tiles = (
        jnp.einsum("tqe,te->tq", tile_block, slot_grads, preferred_element_type=jnp.float32)
        * weight_live[:, None]
    )
    local_grad = (
        jnp.zeros((probs_half.shape[0], block_size), jnp.float32).at[pattern_idx].add(dp_tiles)
    )
    summed_grad = lax.psum(local_grad.reshape(logits.shape), "region")
    logit_grad = probs * (summed_grad - jnp.sum(probs * summed_grad, axis=-1, keepdims=True))
    return (logit_grad, usage_edges.reshape(capacity.shape))


def solution(mesh):
    in_specs = (
        P("nets", None),
        P("nets", "region", None, None, None),
        P("nets", "region", None),
        P("nets", "region", None),
        P("nets", "region", None),
        P("region", "nets"),
    )
    out_specs = (P("nets", None), P("region", "nets"))
    return jax.shard_map(shards, mesh=mesh, in_specs=in_specs, out_specs=out_specs, check_vma=False)
```

profile of v0, /device:TPU:0, one launch (start us, length us, event | category | flops | bytes accessed | tf_op | source)
XLA Modules:
  0.0 181.0 jit_solution(4683535861114849851)
XLA Ops:
  7.2 0.0 reduce-scatter.2.cloned.1.call-start
  7.2 0.7 fusion.17
  7.9 0.7 fusion.18
  8.6 1.4 reduce_max.9
  10.1 1.6 fusion.5
  11.7 0.7 fusion.16
  12.4 0.1 reshape.122
  12.5 1.6 fusion.21
  14.0 0.0 copy-start.1
  14.1 0.2 reshape.119
  14.2 1.4 gather_fusion
  15.7 6.4 %fusion.2 = f32[384,1,128]{2,1,0:T(1,128)S(1)} fusion(bf16[1,1,384,128,128]{4,3,2,1,0:T(8,128)(2,1)} %param.7, bf16[384,128,1]{1,0,2:T(8,128)(2,1)S(1)} %bitcast.18), kind=kOutput, calls=%fused_computation.6 | convolution fusion | flops 12582912 | bytes 12877824 | tf_op jit(solution)/shard_map/tq,tqe->te/dot_general | solution.py:24
  22.1 0.0 copy-start
  22.1 2.6 %scatter_custom_fusion = f32[512,128]{1,0:T(8,128)} fusion(s32[384]{0:T(512)S(1)} %fusion.18, f32[384,128]{1,0:T(8,128)S(1)} %bitcast.19, f32[]{:T(128)} %constant.11.clone.1, f32[384]{0:T(512)S(1)} %reshape.122), kind=kCustom, calls=%fused_computation.18 | custom fusion | flops 98304 | bytes 460804 | tf_op jit(solution)/shard_map/scatter-add | solution.py:32
  24.7 0.0 reduce-scatter.2.cloned.1.call-update
  24.7 0.0 all-reduce.2.cloned.1.call-start
  24.8 0.0 copy-done.1
  24.8 64.0 %reduce-scatter.2.cloned.1.call-done = f32[64,128]{1,0:T(8,128)} async-done(((f32[512,128]{1,0:T(8,128)}), f32[64,128]{1,0:T(8,128)}) %reduce-scatter.2.cloned.1.call-update) | async-done | bytes 32784 | tf_op jit(solution)/shard_map/reduce_scatter | solution.py:34
  88.8 0.8 divide_convert_fusion
  89.6 30.5 %all_gather.3 = bf16[512,128]{1,0:T(8,128)(2,1)S(1)} all-gather(bf16[64,128]{1,0:T(8,128)(2,1)S(1)} %divide_convert_fusion), channel_id=1, replica_groups=mesh['nets'=8,'region'=4] {'nets'}, dimensions={0}, use_global_device_ids=true | all-gather | bytes 147456 | tf_op jit(solution)/shard_map/all_gather | solution.py:36
  120.1 1.4 gather_fusion.1
  121.6 9.5 %fusion = f32[384,1,128]{2,1,0:T(1,128)S(1)} fusion(bf16[1,1,384,128,128]{4,3,2,1,0:T(8,128)(2,1)} %param.7, bf16[384,128,1]{1,0,2:T(8,128)(2,1)S(1)} %bitcast.20), kind=kOutput, calls=%fused_computation.4 | convolution fusion | flops 12582912 | bytes 12877824 | tf_op jit(solution)/shard_map/tqe,te->tq/dot_general | solution.py:39
  131.0 2.2 %scatter_custom_fusion.1 = f32[2048,128]{1,0:T(8,128)S(1)} fusion(s32[384]{0:T(512)S(1)} %fusion.17, f32[]{:T(128)} %constant.11.clone.1, f32[384,128]{1,0:T(8,128)S(1)} %bitcast.21, f32[384]{0:T(512)S(1)} %reshape.122), kind=kCustom, calls=%fused_computation.13 | custom fusion | flops 98304 | bytes 1247236 | tf_op jit(solution)/shard_map/scatter-add | solution.py:43
  133.2 1.3 reshape.120
  134.5 0.0 all-reduce.2.cloned.1.call-update
  134.5 35.3 %all-reduce.2.cloned.1.call-done = f32[1024,256]{1,0:T(8,128)} async-done(((f32[1024,256]{1,0:T(8,128)}), f32[1024,256]{1,0:T(8,128)}) %all-reduce.2.cloned.1.call-update) | async-done | bytes 1048592 | tf_op jit(solution)/shard_map/psum | solution.py:45
  169.8 0.0 copy-done
  169.8 1.7 multiply_reduce_fusion
  171.5 2.7 %subtract_multiply_fusion = f32[1024,256]{1,0:T(8,128)} fusion(f32[1024,256]{1,0:T(8,128)} %all-reduce.2.cloned.1.call-done, f32[1024]{0:T(1024)S(1)} %multiply_reduce_fusion, f32[1024]{0:T(1024)S(1)} %fusion.5, f32[1024,256]{1,0:T(8,128)S(1)} %copy-done, f32[1024]{0:T(1024)S(1)} %reduce_max.9), kind=kLoop, calls=%fused_computation.8 | loop fusion | flops 1048576 | bytes 3158016 | tf_op jit(solution)/shard_map/mul | solution.py:46
  (3 shorter events, 0.0 us)
Async XLA Ops:
  7.2 81.6 %reduce-scatter.2.cloned.1.call-start = ((), (), s32[]{:S(2)}) async-start(), calls=%async_computation.1 | async-start | bytes 294912 | tf_op jit(solution)/shard_map/reduce_scatter | solution.py:34
  14.0 10.7 %copy-start.1 = (s32[1,8192]{1,0:T(1,128)S(1)}, s32[1,8192]{1,0:T(1,128)}, u32[]{:S(2)}) copy-start(s32[1,8192]{1,0:T(1,128)} %param.11) | copy-start | bytes 98308
  22.1 147.8 %copy-start = (f32[1024,256]{1,0:T(8,128)S(1)}, f32[1024,256]{1,0:T(8,128)}, u32[]{:S(2)}) copy-start(f32[1024,256]{1,0:T(8,128)} %param.6) | copy-start | bytes 3145732
  24.7 145.1 %all-reduce.2.cloned.1.call-start = ((), (), s32[]{:S(2)}) async-start(), calls=%async_computation.2 | async-start | bytes 2097152 | tf_op jit(solution)/shard_map/psum | solution.py:45
Sparse Core Ops, SparseCore 0:
  24.8 63.9 reduce-scatter.1
  134.7 35.0 all-reduce.1
where the time goes:
time: 181 us
  waiting for transfers between devices  99.3 us (55%)
  blocking collectives  30.5 us (17%)
  other arithmetic  16.8 us (9%)
  matrix products  15.8 us (9%)
  between operations  14.1 us (8%)
  local copies, waits for them, and re-layouts  4.42 us (2%)
    reduce_scatter x1, waiting for transfers between devices, shards(): lax.psum_scatter(partial_value, 'nets', scatter_dimension=0, tiled=True)  64 us
    psum x1, waiting for transfers between devices, shards(): summed_grad = lax.psum(local_grad.reshape(logits.shape), 'region')  35.3 us
    all_gather x1, blocking collectives, shards(): all_grads = lax.all_gather(edge_grad, 'nets', axis=0, tiled=True)  30.5 us
    dot_general x1, matrix products, shards(): jnp.einsum('tqe,te->tq', tile_block, slot_grads, preferred_element_type=j...  9.46 us
    dot_general x1, matrix products, shards(): jnp.einsum('tq,tqe->te', picked, tile_block, preferred_element_type=jnp.f...  6.35 us
  transfers between devices with their start and end apart: 2, of which 2 were waited for; matrix products, arithmetic and copies ran while one was open for 0% of the time, Pallas kernels for 0%

commit v1 on v0

--- a/solution.py
+++ b/solution.py
@@ -33,7 +33,12 @@
     )
     usage_edges = lax.psum_scatter(partial_value, "nets", scatter_dimension=0, tiled=True)
     edge_grad = jax.nn.sigmoid(usage_edges - capacity_f).astype(jnp.bfloat16)
-    all_grads = lax.all_gather(edge_grad, "nets", axis=0, tiled=True)
+    ring = [edge_grad]
+    for hop in range(7):
+        ring.append(lax.ppermute(ring[-1], "nets", [(dev, (dev + 1) % 8) for dev in range(8)]))
+    all_grads = jnp.roll(
+        jnp.concatenate(ring[::-1], axis=0), (lax.axis_index("nets") + 1) * ring[0].shape[0], axis=0
+    )
     slot_grads = all_grads[target]
     dp_tiles = (
         jnp.einsum("tqe,te->tq", tile_block, slot_grads, preferred_element_type=jnp.float32)

time: 181 us -> 195 us (1.077)
  waiting for transfers between devices: 99.3 us -> 141 us
  blocking collectives: 30.5 us -> 0 us
    ppermute x0 -> x7, waiting for transfers between devices: none -> 43.7 us  [shards(): lax.ppermute(ring[-1], 'nets', [(dev, (dev + 1) % 8) for dev in range(8)])]
    all_gather x1 -> x0, blocking collectives: 30.5 us -> none  [shards(): all_grads = lax.all_gather(edge_grad, 'nets', axis=0, tiled=True)]
  transfers between devices with their start and end apart: 2 -> 9, of which waited for: 2 -> 9; matrix products, arithmetic and copies ran while one was open for 0% -> 0% of each run, Pallas kernels for 0% -> 0%
where the time goes in v1:
time: 195 us; the launch traced here: 194 us
  waiting for transfers between devices  141 us (72%)
  other arithmetic  16.8 us (9%)
  matrix products  15.8 us (8%)
  between operations  14.2 us (7%)
  local copies, waits for them, and re-layouts  4.58 us (2%)
    reduce_scatter x1, waiting for transfers between devices, shards(): lax.psum_scatter(partial_value, 'nets', scatter_dimension=0, tiled=True)  64 us
    ppermute x7, waiting for transfers between devices, shards(): lax.ppermute(ring[-1], 'nets', [(dev, (dev + 1) % 8) for dev in range(8)])  43.7 us
    psum x1, waiting for transfers between devices, shards(): summed_grad = lax.psum(local_grad.reshape(logits.shape), 'region')  33.4 us
    dot_general x1, matrix products, shards(): jnp.einsum('tqe,te->tq', tile_block, slot_grads, preferred_element_type=j...  9.46 us
    dot_general x1, matrix products, shards(): jnp.einsum('tq,tqe->te', picked, tile_block, preferred_element_type=jnp.f...  6.35 us
  transfers between devices with their start and end apart: 9, of which 9 were waited for; matrix products, arithmetic and copies ran while one was open for 0% of the time, Pallas kernels for 0%

profile of v1, /device:TPU:0, one launch (start us, length us, event | category | flops | bytes accessed | tf_op | source)
XLA Modules:
  0.0 194.2 jit_solution(6581640028289121096)
XLA Ops:
  7.2 0.0 reduce-scatter.2.cloned.1.call-start
  7.2 0.7 fusion.17
  7.9 0.7 fusion.18
  8.6 1.4 reduce_max.9
  10.1 1.6 fusion.5
  11.7 0.7 fusion.16
  12.4 0.1 reshape.122
  12.5 1.6 fusion.21
  14.0 0.0 copy-start.1
  14.1 0.2 reshape.119
  14.2 1.4 gather_fusion
  15.7 6.4 %fusion.2 = f32[384,1,128]{2,1,0:T(1,128)S(1)} fusion(bf16[1,1,384,128,128]{4,3,2,1,0:T(8,128)(2,1)} %param.7, bf16[384,128,1]{1,0,2:T(8,128)(2,1)S(1)} %bitcast.18), kind=kOutput, calls=%fused_computation.6 | convolution fusion | flops 12582912 | bytes 12877824 | tf_op jit(solution)/shard_map/tq,tqe->te/dot_general | solution.py:24
  22.1 0.0 copy-start
  22.1 2.6 %scatter_custom_fusion = f32[512,128]{1,0:T(8,128)} fusion(s32[384]{0:T(512)S(1)} %fusion.18, f32[384,128]{1,0:T(8,128)S(1)} %bitcast.19, f32[]{:T(128)} %constant.22.clone.1, f32[384]{0:T(512)S(1)} %reshape.122), kind=kCustom, calls=%fused_computation.18 | custom fusion | flops 98304 | bytes 460804 | tf_op jit(solution)/shard_map/scatter-add | solution.py:32
  24.7 0.0 reduce-scatter.2.cloned.1.call-update
  24.7 0.0 all-reduce.2.cloned.1.call-start
  24.8 0.0 copy-done.1
  24.8 64.0 %reduce-scatter.2.cloned.1.call-done = f32[64,128]{1,0:T(8,128)} async-done(((f32[512,128]{1,0:T(8,128)}), f32[64,128]{1,0:T(8,128)}) %reduce-scatter.2.cloned.1.call-update) | async-done | bytes 32784 | tf_op jit(solution)/shard_map/reduce_scatter | solution.py:34
  88.8 0.8 divide_convert_fusion
  89.6 1.5 collective-permute-start
  91.1 5.0 %collective-permute-done = bf16[64,128]{1,0:T(8,128)(2,1)S(1)} collective-permute-done((bf16[64,128]{1,0:T(8,128)(2,1)S(1)}, bf16[64,128]{1,0:T(8,128)(2,1)S(1)}, u32[]{:S(2)}, u32[]{:S(2)}) %collective-permute-start) | collective-permute-done | bytes 16416 | tf_op jit(solution)/shard_map/ppermute | solution.py:38
  96.1 0.0 collective-permute-start.1
  96.1 6.4 %collective-permute-done.1 = bf16[64,128]{1,0:T(8,128)(2,1)S(1)} collective-permute-done((bf16[64,128]{1,0:T(8,128)(2,1)S(1)}, bf16[64,128]{1,0:T(8,128)(2,1)S(1)}, u32[]{:S(2)}, u32[]{:S(2)}) %collective-permute-start.1) | collective-permute-done | bytes 16416 | tf_op jit(solution)/shard_map/ppermute | solution.py:38
  102.5 0.0 collective-permute-start.2
  102.5 6.6 %collective-permute-done.2 = bf16[64,128]{1,0:T(8,128)(2,1)S(1)} collective-permute-done((bf16[64,128]{1,0:T(8,128)(2,1)S(1)}, bf16[64,128]{1,0:T(8,128)(2,1)S(1)}, u32[]{:S(2)}, u32[]{:S(2)}) %collective-permute-start.2) | collective-permute-done | bytes 16416 | tf_op jit(solution)/shard_map/ppermute | solution.py:38
  109.1 0.0 collective-permute-start.3
  109.1 6.4 %collective-permute-done.3 = bf16[64,128]{1,0:T(8,128)(2,1)S(1)} collective-permute-done((bf16[64,128]{1,0:T(8,128)(2,1)S(1)}, bf16[64,128]{1,0:T(8,128)(2,1)S(1)}, u32[]{:S(2)}, u32[]{:S(2)}) %collective-permute-start.3) | collective-permute-done | bytes 16416 | tf_op jit(solution)/shard_map/ppermute | solution.py:38
  115.5 0.0 collective-permute-start.4
  115.5 6.4 %collective-permute-done.4 = bf16[64,128]{1,0:T(8,128)(2,1)S(1)} collective-permute-done((bf16[64,128]{1,0:T(8,128)(2,1)S(1)}, bf16[64,128]{1,0:T(8,128)(2,1)S(1)}, u32[]{:S(2)}, u32[]{:S(2)}) %collective-permute-start.4) | collective-permute-done | bytes 16416 | tf_op jit(solution)/shard_map/ppermute | solution.py:38
  121.9 0.0 collective-permute-start.5
  121.9 6.4 %collective-permute-done.5 = bf16[64,128]{1,0:T(8,128)(2,1)S(1)} collective-permute-done((bf16[64,128]{1,0:T(8,128)(2,1)S(1)}, bf16[64,128]{1,0:T(8,128)(2,1)S(1)}, u32[]{:S(2)}, u32[]{:S(2)}) %collective-permute-start.5) | collective-permute-done | bytes 16416 | tf_op jit(solution)/shard_map/ppermute | solution.py:38
  128.4 0.0 collective-permute-start.6
  128.4 6.4 %collective-permute-done.6 = bf16[64,128]{1,0:T(8,128)(2,1)S(1)} collective-permute-done((bf16[64,128]{1,0:T(8,128)(2,1)S(1)}, bf16[64,128]{1,0:T(8,128)(2,1)S(1)}, u32[]{:S(2)}, u32[]{:S(2)}) %collective-permute-start.6) | collective-permute-done | bytes 16416 | tf_op jit(solution)/shard_map/ppermute | solution.py:38
  135.0 1.4 gather_fusion.1
  136.5 9.5 %fusion = f32[384,1,128]{2,1,0:T(1,128)S(1)} fusion(bf16[1,1,384,128,128]{4,3,2,1,0:T(8,128)(2,1)} %param.7, bf16[384,128,1]{1,0,2:T(8,128)(2,1)S(1)} %bitcast.20), kind=kOutput, calls=%fused_computation.4 | convolution fusion | flops 12582912 | bytes 12877824 | tf_op jit(solution)/shard_map/tqe,te->tq/dot_general | solution.py:44
  145.9 2.2 %scatter_custom_fusion.1 = f32[2048,128]{1,0:T(8,128)S(1)} fusion(s32[384]{0:T(512)S(1)} %fusion.17, f32[]{:T(128)} %constant.22.clone.1, f32[384,128]{1,0:T(8,128)S(1)} %bitcast.21, f32[384]{0:T(512)S(1)} %reshape.122), kind=kCustom, calls=%fused_computation.13 | custom fusion | flops 98304 | bytes 1247236 | tf_op jit(solution)/shard_map/scatter-add | solution.py:48
  148.2 1.3 reshape.120
  149.4 0.0 all-reduce.2.cloned.1.call-update
  149.5 33.4 %all-reduce.2.cloned.1.call-done = f32[1024,256]{1,0:T(8,128)} async-done(((f32[1024,256]{1,0:T(8,128)}), f32[1024,256]{1,0:T(8,128)}) %all-reduce.2.cloned.1.call-update) | async-done | bytes 1048592 | tf_op jit(solution)/shard_map/psum | solution.py:50
  182.9 0.0 copy-done
  182.9 1.7 multiply_reduce_fusion
  184.6 2.7 %subtract_multiply_fusion = f32[1024,256]{1,0:T(8,128)} fusion(f32[1024,256]{1,0:T(8,128)} %all-reduce.2.cloned.1.call-done, f32[1024]{0:T(1024)S(1)} %multiply_reduce_fusion, f32[1024]{0:T(1024)S(1)} %fusion.5, f32[1024,256]{1,0:T(8,128)S(1)} %copy-done, f32[1024]{0:T(1024)S(1)} %reduce_max.9), kind=kLoop, calls=%fused_computation.8 | loop fusion | flops 1048576 | bytes 3158016 | tf_op jit(solution)/shard_map/mul | solution.py:51
  (20 shorter events, 0.2 us)
Async XLA Ops:
  7.2 81.6 %reduce-scatter.2.cloned.1.call-start = ((), (), s32[]{:S(2)}) async-start(), calls=%async_computation.1 | async-start | bytes 294912 | tf_op jit(solution)/shard_map/reduce_scatter | solution.py:34
  14.0 10.7 %copy-start.1 = (s32[1,8192]{1,0:T(1,128)S(1)}, s32[1,8192]{1,0:T(1,128)}, u32[]{:S(2)}) copy-start(s32[1,8192]{1,0:T(1,128)} %param.11) | copy-start | bytes 98308
  22.1 160.9 %copy-start = (f32[1024,256]{1,0:T(8,128)S(1)}, f32[1024,256]{1,0:T(8,128)}, u32[]{:S(2)}) copy-start(f32[1024,256]{1,0:T(8,128)} %param.6) | copy-start | bytes 3145732
  24.7 158.2 %all-reduce.2.cloned.1.call-start = ((), (), s32[]{:S(2)}) async-start(), calls=%async_computation.2 | async-start | bytes 2097152 | tf_op jit(solution)/shard_map/psum | solution.py:50
  89.6 6.5 %collective-permute-start = (bf16[64,128]{1,0:T(8,128)(2,1)S(1)}, bf16[64,128]{1,0:T(8,128)(2,1)S(1)}, u32[]{:S(2)}, u32[]{:S(2)}) collective-permute-start(bf16[64,128]{1,0:T(8,128)(2,1)S(1)} %divide_convert_fusion), channel_id=1, source_target_pairs={{0,4},{4,8},{8,12},{12,16},{16,20},{20,24},{24,28},{28,0},{1,5},{5... | collective-permute-start | bytes 49160 | tf_op jit(solution)/shard_map/ppermute | solution.py:38
  96.1 6.4 %collective-permute-start.1 = (bf16[64,128]{1,0:T(8,128)(2,1)S(1)}, bf16[64,128]{1,0:T(8,128)(2,1)S(1)}, u32[]{:S(2)}, u32[]{:S(2)}) collective-permute-start(bf16[64,128]{1,0:T(8,128)(2,1)S(1)} %collective-permute-done), channel_id=1, source_target_pairs={{0,4},{4,8},{8,12},{12,16},{16,20},{20,24},{24,28},{28,0},{1,5},{5... | collective-permute-start | bytes 49160 | tf_op jit(solution)/shard_map/ppermute | solution.py:38
  102.5 6.6 %collective-permute-start.2 = (bf16[64,128]{1,0:T(8,128)(2,1)S(1)}, bf16[64,128]{1,0:T(8,128)(2,1)S(1)}, u32[]{:S(2)}, u32[]{:S(2)}) collective-permute-start(bf16[64,128]{1,0:T(8,128)(2,1)S(1)} %collective-permute-done.1), channel_id=1, source_target_pairs={{0,4},{4,8},{8,12},{12,16},{16,20},{20,24},{24,28},{28,0},{1,5},{5... | collective-permute-start | bytes 49160 | tf_op jit(solution)/shard_map/ppermute | solution.py:38
  109.1 6.4 %collective-permute-start.3 = (bf16[64,128]{1,0:T(8,128)(2,1)S(1)}, bf16[64,128]{1,0:T(8,128)(2,1)S(1)}, u32[]{:S(2)}, u32[]{:S(2)}) collective-permute-start(bf16[64,128]{1,0:T(8,128)(2,1)S(1)} %collective-permute-done.2), channel_id=1, source_target_pairs={{0,4},{4,8},{8,12},{12,16},{16,20},{20,24},{24,28},{28,0},{1,5},{5... | collective-permute-start | bytes 49160 | tf_op jit(solution)/shard_map/ppermute | solution.py:38
  115.5 6.4 %collective-permute-start.4 = (bf16[64,128]{1,0:T(8,128)(2,1)S(1)}, bf16[64,128]{1,0:T(8,128)(2,1)S(1)}, u32[]{:S(2)}, u32[]{:S(2)}) collective-permute-start(bf16[64,128]{1,0:T(8,128)(2,1)S(1)} %collective-permute-done.3), channel_id=1, source_target_pairs={{0,4},{4,8},{8,12},{12,16},{16,20},{20,24},{24,28},{28,0},{1,5},{5... | collective-permute-start | bytes 49160 | tf_op jit(solution)/shard_map/ppermute | solution.py:38
  121.9 6.4 %collective-permute-start.5 = (bf16[64,128]{1,0:T(8,128)(2,1)S(1)}, bf16[64,128]{1,0:T(8,128)(2,1)S(1)}, u32[]{:S(2)}, u32[]{:S(2)}) collective-permute-start(bf16[64,128]{1,0:T(8,128)(2,1)S(1)} %collective-permute-done.4), channel_id=1, source_target_pairs={{0,4},{4,8},{8,12},{12,16},{16,20},{20,24},{24,28},{28,0},{1,5},{5... | collective-permute-start | bytes 49160 | tf_op jit(solution)/shard_map/ppermute | solution.py:38
  128.4 6.4 %collective-permute-start.6 = (bf16[64,128]{1,0:T(8,128)(2,1)S(1)}, bf16[64,128]{1,0:T(8,128)(2,1)S(1)}, u32[]{:S(2)}, u32[]{:S(2)}) collective-permute-start(bf16[64,128]{1,0:T(8,128)(2,1)S(1)} %collective-permute-done.5), channel_id=1, source_target_pairs={{0,4},{4,8},{8,12},{12,16},{16,20},{20,24},{24,28},{28,0},{1,5},{5... | collective-permute-start | bytes 49160 | tf_op jit(solution)/shard_map/ppermute | solution.py:38
Sparse Core Ops, SparseCore 0:
  24.8 63.9 reduce-scatter.1
  149.6 33.2 all-reduce.1
